TPU v7x, 128 devices: a whole 4x4x4 slice. The times are simulated.
128 devices in a mesh: sub: 128 (over z, y, x, core).
Axes of the slice: x: 4, y: 4, z: 4, core: 2. Of those that a mesh axis runs over, the one named last changes fastest.
Arguments:
- pool_inputs: bfloat16 [65536, 4096], P('sub'), may hold values from -6 to 6
- pool_targets: bfloat16 [65536, 4096], P('sub'), may hold values from -6 to 6
- row_picks: int32 [8, 32768], P(None, 'sub'), may hold values from 0 to 511
- weight_in: float32 [4096, 32768], P(None, 'sub'), may hold values from -6 to 6
- weight_out: float32 [4096, 32768], P(None, 'sub'), may hold values from -6 to 6
- eval_inputs: bfloat16 [256, 4096], P('sub'), may hold values from -6 to 6
- handover: int32 [4096], replicated, may hold values from 0 to 4095, as said below
Outputs:
- trained_in: float32 [4096, 32768], P(None, 'sub')
- trained_out: float32 [4096, 32768], P(None, 'sub')
- prediction: float32 [256, 4096], P('sub')
Inputs may be any that keep to these rules, and one draw needn't show every extreme that they name: `row_picks`: indices into the subnet's own 512 resident rows. handover[g] is the new position of neuron group g (neurons 8 g to 8 g + 7); every position is taken once, and no two groups of one subnet move to the same subnet.
All inputs are finite; a program needn't handle non-finite values.
Results may differ from a plain program's by a relative error of at most 0.0065.
Values may be sent and summed in bfloat16 or wider, within the bound.
No kernel may reach another device: no remote copies, remote signals or barrier semaphores. Data moves between devices by JAX's collectives and lax.ppermute only.
A program may use at most 192 MiB of HBM per device.

v0:
```python
import math
import jax
import jax.numpy as jnp
from jax import lax
from jax.sharding import PartitionSpec as P

D = 4096
GROUP = 8
STEPS = 4
tanh_coef = 0.7978845608028654
cubic_coef = 0.044715
step_rate = 0.5


def gelu_value(inputs):
    inner_term = tanh_coef * (inputs + cubic_coef * inputs * inputs * inputs)
    return 0.5 * inputs * (1.0 + jnp.tanh(inner_term))


def gelu_parts(inputs):
    tanh_part = jnp.tanh(tanh_coef * (inputs + cubic_coef * inputs * inputs * inputs))
    values = 0.5 * inputs * (1.0 + tanh_part)
    slopes = 0.5 * (1.0 + tanh_part) + 0.5 * inputs * (1.0 - tanh_part * tanh_part) * tanh_coef * (
        1.0 + 3.0 * cubic_coef * inputs * inputs
    )
    return (values, slopes)


def train_step(layer_in, layer_out, batch_rows, batch_goals, scale_in, scale_out):
    in_half = layer_in.astype(jnp.bfloat16)
    out_half = layer_out.astype(jnp.bfloat16)
    before = jnp.dot(batch_rows, in_half, preferred_element_type=jnp.float32) * scale_in
    values, slopes = gelu_parts(before)
    activity = values.astype(jnp.bfloat16)
    branch = jnp.dot(activity, out_half.T, preferred_element_type=jnp.float32) * scale_out
    errors = (branch - batch_goals.astype(jnp.float32)).astype(jnp.bfloat16)
    grad_out = jnp.dot(errors.T, activity, preferred_element_type=jnp.float32) * scale_out
    backward = (
        jnp.dot(errors, out_half, preferred_element_type=jnp.float32) * scale_out * slopes
    ).astype(jnp.bfloat16)
    grad_in = jnp.dot(batch_rows.T, backward, preferred_element_type=jnp.float32) * scale_in
    return (layer_in - step_rate * grad_in, layer_out - step_rate * grad_out)


def local_round(
    layer_in, layer_out, pool_inputs, pool_targets, row_picks, first_turn, scale_in, scale_out
):

    def one_turn(turn_index, carry):
        current_in, current_out = carry
        picked = lax.dynamic_slice_in_dim(row_picks, first_turn + turn_index, 1, 0)[0]
        batch_rows = jnp.take(pool_inputs, picked, axis=0)
        batch_goals = jnp.take(pool_targets, picked, axis=0)
        return train_step(current_in, current_out, batch_rows, batch_goals, scale_in, scale_out)

    return lax.fori_loop(0, STEPS, one_turn, (layer_in, layer_out))


def per_device(pool_inputs, pool_targets, row_picks, weight_in, weight_out, eval_inputs, handover):
    owners = lax.axis_size("sub")
    my_index = lax.axis_index("sub")
    hidden = weight_in.shape[1]
    group_count = hidden // GROUP
    total_groups = group_count * owners
    scale_in = 1.0 / math.sqrt(D)
    scale_out = 1.0 / math.sqrt(hidden * owners)
    layer_in, layer_out = local_round(
        weight_in, weight_out, pool_inputs, pool_targets, row_picks, 0, scale_in, scale_out
    )
    in_half = layer_in.astype(jnp.bfloat16)
    out_half = layer_out.astype(jnp.bfloat16)
    eval_act = gelu_value(
        jnp.dot(
            lax.all_gather(eval_inputs, "sub", axis=0, tiled=True),
            in_half,
            preferred_element_type=jnp.float32,
        )
        * scale_in
    ).astype(jnp.bfloat16)
    prediction = lax.psum_scatter(
        jnp.dot(eval_act, out_half.T, preferred_element_type=jnp.float32) * scale_out,
        "sub",
        scatter_dimension=0,
        tiled=True,
    )
    inverse = (
        jnp.zeros((total_groups,), jnp.int32)
        .at[handover]
        .set(jnp.arange(total_groups, dtype=jnp.int32))
    )
    offsets = jnp.arange(GROUP, dtype=jnp.int32)
    local_groups = lax.dynamic_slice_in_dim(handover, my_index * group_count, group_count, 0)
    targets = local_groups // group_count
    matches = targets[None, :] == jnp.arange(owners, dtype=jnp.int32)[:, None]
    chosen_group = jnp.sum(
        jnp.where(matches, jnp.arange(group_count, dtype=jnp.int32)[None, :], 0), axis=1
    )
    send_columns = (chosen_group[:, None] * GROUP + offsets[None, :]).reshape(-1)
    outgoing_in = jnp.take(layer_in, send_columns, axis=1)
    outgoing_out = jnp.take(layer_out, send_columns, axis=1)
    landed_in, landed_out = (
        lax.all_to_all(outgoing_in, "sub", split_axis=1, concat_axis=1, tiled=True),
        lax.all_to_all(outgoing_out, "sub", split_axis=1, concat_axis=1, tiled=True),
    )
    arriving = lax.dynamic_slice_in_dim(inverse, my_index * group_count, group_count, 0)
    sources = arriving // group_count
    take_columns = (sources[:, None] * GROUP + offsets[None, :]).reshape(-1)
    handed_in = jnp.take(landed_in, take_columns, axis=1)
    handed_out = jnp.take(landed_out, take_columns, axis=1)
    trained_in, trained_out = local_round(
        handed_in, handed_out, pool_inputs, pool_targets, row_picks, STEPS, scale_in, scale_out
    )
    return (trained_in, trained_out, prediction)


def solution(mesh):
    in_specs = (
        P("sub", None),
        P("sub", None),
        P(None, "sub"),
        P(None, "sub"),
        P(None, "sub"),
        P("sub", None),
        P(),
    )
    out_specs = (P(None, "sub"), P(None, "sub"), P("sub", None))
    return jax.shard_map(
        per_device, mesh=mesh, in_specs=in_specs, out_specs=out_specs, check_vma=False
    )
```

profile of v0, /device:TPU:1, one launch (start us, length us, event | category | flops | bytes accessed | tf_op | source)
XLA Modules:
  0.0 1054.3 jit_solution(7046368642467714534)
XLA Ops:
  13.8 15.5 %scatter_custom_fusion = s32[4096]{0:T(1024)S(1)} fusion(s32[4096]{0:T(1024)S(1)} %compare_select_fusion.2, s32[4096]{0:T(1024)S(1)} %iota.16, s32[]{:T(128)} %constant.305.clone.1), kind=kCustom, calls=%fused_computation.142 | custom fusion | bytes 16388 | tf_op jit(solution)/shard_map/scatter | solution.py:89
  30.9 157.9 %while.36 = (s32[]{:T(128)}, f32[4096,256]{1,0:T(8,128)}, f32[4096,256]{1,0:T(8,128)}, s32[8,256]{1,0:T(8,128)}, bf16[512,4096]{1,0:T(8,128)(2,1)}, /*index=5*/bf16[512,4096]{1,0:T(8,128)(2,1)}, s32[]{:T(128)}) while((s32[]{:T(128)}, f32[4096,256]{1,0:T(8,128)}, f32[4096,256]{1,0:T(8,128)}, s32[8,256]{1,0:T(8,128)}, ...), condition=%wide.region_1.3_spmd, body=%wide.region_0.2_spmd.sunk | while | flops 2701724928 | bytes 59782260 | solution.py:56
  31.6 6.6 gather_fusion.1
  42.0 7.9 gather_fusion
  53.7 8.6 fusion.148
  68.1 6.6 gather_fusion.1
  78.5 7.9 gather_fusion
  90.2 8.6 fusion.148
  104.7 6.6 gather_fusion.1
  115.0 7.9 gather_fusion
  126.8 8.6 fusion.148
  151.5 7.9 gather_fusion
  163.3 8.6 fusion.148
  200.2 16.8 %gather_fusion.6 = f32[1024,4096]{1,0:T(8,128)} fusion(f32[4096,256]{0,1:T(8,128)} %copy.23, s32[1024]{0:T(1024)S(1)} %fusion.111), kind=kCustom, calls=%fused_computation.6.clone | custom fusion | bytes 33558528 | tf_op jit(solution)/shard_map/jit(_take)/gather | solution.py:100
  217.0 16.8 %gather_fusion.4 = f32[1024,4096]{1,0:T(8,128)} fusion(f32[4096,256]{0,1:T(8,128)} %copy.22, s32[1024]{0:T(1024)S(1)} %fusion.111), kind=kCustom, calls=%fused_computation.1.clone | custom fusion | bytes 33558528 | tf_op jit(solution)/shard_map/jit(_take)/gather | solution.py:99
  233.8 16.9 %select_bitcast_fusion = (f32[4096,128,8]{0,2,1:T(8,128)S(1)}, f32[4096,128,8]{0,2,1:T(8,128)}) fusion(f32[1024,4096]{1,0:T(8,128)} %gather_fusion.6, pred[1024]{0:T(1024)(128)(4,1)S(1)} %copy-done.4, f32[1024,4096]{1,0:T(8,128)} %gather_fusion.4), kind=kLoop, calls=%fused_computation.117 | loop fusion | flops 8388608 | bytes 67109888 | tf_op jit(solution)/shard_map/all_to_all | solution.py:103
  250.7 199.2 %all_to_all.24 = f32[4096,128,8]{0,2,1:T(8,128)} all-to-all(f32[4096,128,8]{0,2,1:T(8,128)S(1)} %get-tuple-element.425), channel_id=1, replica_groups=mesh['sub'=128] {'sub'}, dimensions={1} | all-to-all | bytes 33554432 | tf_op jit(solution)/shard_map/all_to_all | solution.py:103
  456.4 235.1 %all-gather.3.cloned.1.call-done = bf16[128,2,4096]{2,1,0:T(2,128)(2,1)} async-done(((bf16[1,2,4096]{2,1,0:T(2,128)(2,1)}), bf16[128,2,4096]{2,1,0:T(2,128)(2,1)}) %all-gather.3.cloned.1.call-update) | async-done | bytes 2097168 | tf_op jit(solution)/shard_map/all_gather | solution.py:74
  694.3 8.0 convolution_multiply_fusion.8
  703.1 153.8 %all-reduce.3.cloned.1.call-done = f32[256,4096]{1,0:T(8,128)} async-done(((f32[256,4096]{1,0:T(8,128)}), f32[256,4096]{1,0:T(8,128)}) %all-reduce.3.cloned.1.call-update) | async-done | bytes 4194320
  858.5 11.5 %gather_fusion.7 = f32[256,4096]{1,0:T(8,128)} fusion(f32[4096,1024]{0,1:T(8,128)} %bitcast.47, s32[1024]{0:T(1024)S(1)} %pad_clamp_fusion.2), kind=kCustom, calls=%fused_computation.7.clone | custom fusion | bytes 8389632 | tf_op jit(solution)/shard_map/jit(_take)/gather | solution.py:109
  870.0 11.5 %gather_fusion.5 = f32[256,4096]{1,0:T(8,128)} fusion(f32[4096,1024]{0,1:T(8,128)} %bitcast.4, s32[1024]{0:T(1024)S(1)} %pad_clamp_fusion.2), kind=kCustom, calls=%fused_computation.2.clone | custom fusion | bytes 8389632 | tf_op jit(solution)/shard_map/jit(_take)/gather | solution.py:108
  881.5 8.4 select_bitcast_fusion.2
  901.1 146.0 %while.37 = (s32[]{:T(128)}, f32[4096,256]{1,0:T(8,128)}, f32[4096,256]{1,0:T(8,128)}, s32[8,256]{1,0:T(8,128)}, bf16[512,4096]{1,0:T(8,128)(2,1)}, /*index=5*/b...) while((s32[]{:T(128)}, f32[4096,256]{1,0:T(8,128)}, f32[4096,256]{1,0:T(8,128)}, ...), condition=%wide.region_5.9_spmd, body=%wide.region_4.8_spmd.sunk | while | flops 2701724928 | bytes 59782328 | solution.py:56
  912.2 7.9 gather_fusion.2
  923.9 8.6 fusion.157
  948.7 7.9 gather_fusion.2
  960.4 8.6 fusion.157
  985.2 7.9 gather_fusion.2
  996.9 8.6 fusion.157
  1021.7 7.9 gather_fusion.2
  1033.4 8.6 fusion.157
  (113 shorter events, 181.9 us)
Async XLA Ops:
  7.2 4.6 copy-start.2
  11.8 2.0 copy-start.3
  38.3 3.7 copy-start
  74.8 3.7 copy-start
  111.3 3.7 copy-start
  147.8 3.7 copy-start
  217.0 16.8 %copy-start.4 = (pred[1024]{0:T(1024)(128)(4,1)S(1)}, pred[1024]{0:T(1024)(128)(4,1)}, u32[]{:S(2)}) copy-start(pred[1024]{0:T(1024)(128)(4,1)} %compare_and_fusion.2) | copy-start | bytes 3076
  449.9 420.0 %all-to-all-start = ((f32[4096,128,8]{0,2,1:T(8,128)}), f32[4096,128,8]{0,2,1:T(8,128)}, u32[]{:S(2)}, u32[]{:S(2)}) async-start(f32[4096,128,8]{0,2,1:T(8,128)} %get-tuple-element.426), calls=%async_computation | async-start | bytes 33554432 | tf_op jit(solution)/shard_map/all_to_all | solution.py:102
  455.6 235.9 %all-gather.3.cloned.1.call-start = ((), (), s32[]{:S(2)}) async-start(), calls=%async_computation.2 | async-start | bytes 2113536 | tf_op jit(solution)/shard_map/all_gather | solution.py:74
  456.4 400.6 %all-reduce.3.cloned.1.call-start = ((), (), s32[]{:S(2)}) async-start(), calls=%async_computation.3 | async-start | bytes 8388608
  702.2 0.7 copy-start.5
  908.4 3.7 copy-start.1
  944.9 3.7 copy-start.1
  981.5 3.7 copy-start.1
  1018.0 3.7 copy-start.1
Sparse Core Ops, SparseCore 0:
  459.6 231.8 all-gather.2
  702.4 154.5 all-reduce.2
where the time goes:
time: 1070 us; the launch traced here: 1050 us
  waiting for transfers between devices  390 us (36%)
  local copies, waits for them, and re-layouts  228 us (21%)
  blocking collectives  199 us (19%)
  matrix products  177 us (17%)
  other arithmetic  27 us (3%)
  between operations  14.5 us (1%)
  loops' own time  12.4 us (1%)
    all_gather x1, waiting for transfers between devices, per_device(): lax.all_gather(eval_inputs, 'sub', axis=0, tiled=True)  235 us
    all_to_all x1, blocking collectives, per_device(): lax.all_to_all(outgoing_out, 'sub', split_axis=1, concat_axis=1, tiled=True)  199 us
    unnamed x3, waiting for transfers between devices  155 us
    dot_general x8, matrix products, train_step(): jnp.dot(batch_rows.T, backward, preferred_element_type=jnp.float32)  68.7 us
    gather x8, local copies, waits for them, and re-layouts, one_turn(): batch_goals = jnp.take(pool_targets, picked, axis=0)  63.4 us
    gather x8, local copies, waits for them, and re-layouts, one_turn(): batch_rows = jnp.take(pool_inputs, picked, axis=0)  52.9 us
    dot_general x8, matrix products, train_step(): jnp.dot(errors.T, activity, preferred_element_type=jnp.float32) * scale_out  40.7 us
    dot_general x8, matrix products, train_step(): jnp.dot(activity, out_half.T, preferred_element_type=jnp.float32)  30.4 us
  transfers between devices with their start and end apart: 3, of which 2 were waited for; matrix products, arithmetic and copies ran while one was open for 2% of the time, Pallas kernels for 0%

commit v1 on v0

--- a/solution.py
+++ b/solution.py
@@ -1,3 +1,4 @@
+import functools
 import math
 import jax
 import jax.numpy as jnp
@@ -10,6 +11,17 @@
 tanh_coef = 0.7978845608028654
 cubic_coef = 0.044715
 step_rate = 0.5
+
+
+def _build_chains(packet, mesh_ax):
+    crops = []
+    for _ in range(lax.axis_size(mesh_ax)):
+        crops.append(packet)
+    res = jnp.stack(crops, 0)
+    return jnp.concatenate(lax.all_to_all(res, mesh_ax, split_axis=0, concat_axis=0), 0)
+
+
+packet_mix = functools.partial(_build_chains, mesh_ax="sub")
 
 
 def gelu_value(inputs):
@@ -70,12 +82,7 @@
     in_half = layer_in.astype(jnp.bfloat16)
     out_half = layer_out.astype(jnp.bfloat16)
     eval_act = gelu_value(
-        jnp.dot(
-            lax.all_gather(eval_inputs, "sub", axis=0, tiled=True),
-            in_half,
-            preferred_element_type=jnp.float32,
-        )
-        * scale_in
+        jnp.dot(packet_mix(eval_inputs), in_half, preferred_element_type=jnp.float32) * scale_in
     ).astype(jnp.bfloat16)
     prediction = lax.psum_scatter(
         jnp.dot(eval_act, out_half.T, preferred_element_type=jnp.float32) * scale_out,

time: 1070 us -> 1020 us (0.953)
  waiting for transfers between devices: 390 us -> 327 us
  starting transfers between devices: 5.74 us -> 17.7 us
    all_gather x1 -> x0, waiting for transfers between devices: 235 us -> none  [per_device(): lax.all_gather(eval_inputs, 'sub', axis=0, tiled=True)]
    unnamed x3 -> x2, waiting for transfers between devices: 155 us -> 327 us
    all_to_all x0 -> x1, starting transfers between devices: none -> 12 us  [_build_chains(): lax.all_to_all(res, mesh_ax, split_axis=0, concat_axis=0)]
  transfers between devices with their start and end apart: 3 -> 3, of which waited for: 2 -> 1; matrix products, arithmetic and copies ran while one was open for 2% -> 25% of each run, Pallas kernels for 0% -> 0%
where the time goes in v1:
time: 1020 us; the launch traced here: 1010 us
  waiting for transfers between devices  327 us (32%)
  local copies, waits for them, and re-layouts  232 us (23%)
  blocking collectives  198 us (19%)
  matrix products  177 us (17%)
  other arithmetic  31.8 us (3%)
  starting transfers between devices  17.7 us (2%)
  between operations  14.4 us (1%)
  loops' own time  12.7 us (1%)
    unnamed x2, waiting for transfers between devices  327 us
    all_to_all x1, blocking collectives, per_device(): lax.all_to_all(outgoing_out, 'sub', split_axis=1, concat_axis=1, tiled=True)  198 us
    dot_general x8, matrix products, train_step(): jnp.dot(batch_rows.T, backward, preferred_element_type=jnp.float32)  68.7 us
    gather x8, local copies, waits for them, and re-layouts, one_turn(): batch_goals = jnp.take(pool_targets, picked, axis=0)  63.4 us
    gather x8, local copies, waits for them, and re-layouts, one_turn(): batch_rows = jnp.take(pool_inputs, picked, axis=0)  52.9 us
    dot_general x8, matrix products, train_step(): jnp.dot(errors.T, activity, preferred_element_type=jnp.float32) * scale_out  40.7 us
    dot_general x8, matrix products, train_step(): jnp.dot(activity, out_half.T, preferred_element_type=jnp.float32)  30.4 us
    dot_general x8, matrix products, train_step(): jnp.dot(batch_rows, in_half, preferred_element_type=jnp.float32) * scale_in  29.6 us
  transfers between devices with their start and end apart: 3, of which 1 were waited for; matrix products, arithmetic and copies ran while one was open for 25% of the time, Pallas kernels for 0%

profile of v1, /device:TPU:1, one launch (start us, length us, event | category | flops | bytes accessed | tf_op | source)
XLA Modules:
  0.0 1010.3 jit_solution(4689772001606844006)
XLA Ops:
  17.3 12.0 %all-to-all-start.2 = ((bf16[128,2,4096]{2,1,0:T(2,128)(2,1)}), bf16[128,2,4096]{2,1,0:T(2,128)(2,1)}, u32[]{:S(2)}, u32[]{:S(2)}) async-start(bf16[128,2,4096]{2,1,0:T(2,128)(2,1)} %stack.2), calls=%async_computation.2 | async-start | bytes 4194304 | tf_op jit(solution)/shard_map/all_to_all | solution.py:21
  29.3 15.5 %scatter_custom_fusion = s32[4096]{0:T(1024)S(1)} fusion(s32[4096]{0:T(1024)S(1)} %compare_select_fusion.2, s32[4096]{0:T(1024)S(1)} %iota.16, s32[]{:T(128)} %constant.305.clone.1), kind=kCustom, calls=%fused_computation.142 | custom fusion | bytes 16388 | tf_op jit(solution)/shard_map/scatter | solution.py:96
  46.4 158.3 %while.36 = (s32[]{:T(128)}, f32[4096,256]{1,0:T(8,128)}, f32[4096,256]{1,0:T(8,128)}, s32[8,256]{1,0:T(8,128)}, bf16[512,4096]{1,0:T(8,128)(2,1)}, /*index=5*/bf16[512,4096]{1,0:T(8,128)(2,1)}, s32[]{:T(128)}) while((s32[]{:T(128)}, f32[4096,256]{1,0:T(8,128)}, f32[4096,256]{1,0:T(8,128)}, s32[8,256]{1,0:T(8,128)}, ...), condition=%wide.region_1.3_spmd, body=%wide.region_0.2_spmd.sunk | while | flops 2701724928 | bytes 59782260 | solution.py:68
  47.5 6.6 gather_fusion.1
  57.8 7.9 gather_fusion
  69.5 8.6 fusion.148
  94.3 7.9 gather_fusion
  106.0 8.6 fusion.148
  120.5 6.6 gather_fusion.1
  130.8 7.9 gather_fusion
  142.6 8.6 fusion.148
  157.0 6.6 gather_fusion.1
  167.3 7.9 gather_fusion
  179.1 8.6 fusion.148
  215.9 16.8 %gather_fusion.6 = f32[1024,4096]{1,0:T(8,128)} fusion(f32[4096,256]{0,1:T(8,128)} %copy.23, s32[1024]{0:T(1024)S(1)} %fusion.111), kind=kCustom, calls=%fused_computation.6.clone | custom fusion | bytes 33558528 | tf_op jit(solution)/shard_map/jit(_take)/gather | solution.py:107
  232.8 16.8 %gather_fusion.4 = f32[1024,4096]{1,0:T(8,128)} fusion(f32[4096,256]{0,1:T(8,128)} %copy.22, s32[1024]{0:T(1024)S(1)} %fusion.111), kind=kCustom, calls=%fused_computation.1.clone | custom fusion | bytes 33558528 | tf_op jit(solution)/shard_map/jit(_take)/gather | solution.py:106
  249.6 21.7 %select_bitcast_fusion = (f32[4096,128,8]{0,2,1:T(8,128)}, f32[4096,128,8]{0,2,1:T(8,128)}) fusion(f32[1024,4096]{1,0:T(8,128)} %gather_fusion.6, pred[1024]{0:T(1024)(128)(4,1)S(1)} %copy-done.5, f32[1024,4096]{1,0:T(8,128)} %gather_fusion.4), kind=kLoop, calls=%fused_computation.117 | loop fusion | flops 8388608 | bytes 67109888 | tf_op jit(solution)/shard_map/all_to_all | solution.py:110
  271.3 197.7 %all_to_all.29 = f32[4096,128,8]{0,2,1:T(8,128)} all-to-all(f32[4096,128,8]{0,2,1:T(8,128)} %get-tuple-element.425), channel_id=1, replica_groups=mesh['sub'=128] {'sub'}, dimensions={1} | all-to-all | bytes 33554432 | tf_op jit(solution)/shard_map/all_to_all | solution.py:110
  477.5 8.0 convolution_multiply_fusion.8
  486.3 326.8 %all-reduce.3.cloned.1.call-done = f32[256,4096]{1,0:T(8,128)} async-done(((f32[256,4096]{1,0:T(8,128)}), f32[256,4096]{1,0:T(8,128)}) %all-reduce.3.cloned.1.call-update) | async-done | bytes 4194320
  814.6 11.5 %gather_fusion.7 = f32[256,4096]{1,0:T(8,128)} fusion(f32[4096,1024]{0,1:T(8,128)} %bitcast.46, s32[1024]{0:T(1024)S(1)} %pad_clamp_fusion.2), kind=kCustom, calls=%fused_computation.7.clone | custom fusion | bytes 8389632 | tf_op jit(solution)/shard_map/jit(_take)/gather | solution.py:116
  826.1 11.5 %gather_fusion.5 = f32[256,4096]{1,0:T(8,128)} fusion(f32[4096,1024]{0,1:T(8,128)} %bitcast.4, s32[1024]{0:T(1024)S(1)} %pad_clamp_fusion.2), kind=kCustom, calls=%fused_computation.2.clone | custom fusion | bytes 8389632 | tf_op jit(solution)/shard_map/jit(_take)/gather | solution.py:115
  837.6 8.4 select_bitcast_fusion.2
  857.2 146.0 %while.37 = (s32[]{:T(128)}, f32[4096,256]{1,0:T(8,128)}, f32[4096,256]{1,0:T(8,128)}, s32[8,256]{1,0:T(8,128)}, bf16[512,4096]{1,0:T(8,128)(2,1)}, /*index=5*/b...) while((s32[]{:T(128)}, f32[4096,256]{1,0:T(8,128)}, f32[4096,256]{1,0:T(8,128)}, ...), condition=%wide.region_5.9_spmd, body=%wide.region_4.8_spmd.sunk | while | flops 2701724928 | bytes 59782328 | solution.py:68
  868.3 7.9 gather_fusion.2
  880.0 8.6 fusion.157
  904.8 7.9 gather_fusion.2
  916.5 8.6 fusion.157
  941.3 7.9 gather_fusion.2
  953.0 8.6 fusion.157
  977.8 7.9 gather_fusion.2
  989.5 8.6 fusion.157
  (115 shorter events, 184.6 us)
Async XLA Ops:
  7.2 4.6 copy-start.2
  11.8 2.0 copy-start.4
  13.8 15.4 %copy-start.3 = (s32[4096]{0:T(1024)S(1)}, s32[4096]{0:T(1024)}, u32[]{:S(2)}) copy-start(s32[4096]{0:T(1024)} %param.23) | copy-start | bytes 49156
  17.3 254.0 %all-to-all-start.2 = ((bf16[128,2,4096]{2,1,0:T(2,128)(2,1)}), bf16[128,2,4096]{2,1,0:T(2,128)(2,1)}, u32[]{:S(2)}, u32[]{:S(2)}) async-start(bf16[128,2,4096]{2,1,0:T(2,128)(2,1)} %stack.2), calls=%async_computation.2 | async-start | bytes 4194304 | tf_op jit(solution)/shard_map/all_to_all | solution.py:21
  54.1 3.7 copy-start
  90.6 3.7 copy-start
  127.1 3.7 copy-start
  163.6 3.7 copy-start
  232.8 16.8 %copy-start.5 = (pred[1024]{0:T(1024)(128)(4,1)S(1)}, pred[1024]{0:T(1024)(128)(4,1)}, u32[]{:S(2)}) copy-start(pred[1024]{0:T(1024)(128)(4,1)} %compare_and_fusion.2) | copy-start | bytes 3076
  469.0 357.1 %all-to-all-start = ((f32[4096,128,8]{0,2,1:T(8,128)}), f32[4096,128,8]{0,2,1:T(8,128)}, u32[]{:S(2)}, u32[]{:S(2)}) async-start(f32[4096,128,8]{0,2,1:T(8,128)} %get-tuple-element.426), calls=%async_computation | async-start | bytes 33554432 | tf_op jit(solution)/shard_map/all_to_all | solution.py:109
  474.7 338.4 %all-reduce.3.cloned.1.call-start = ((), (), s32[]{:S(2)}) async-start(), calls=%async_computation.3 | async-start | bytes 8388608
  485.4 0.7 copy-start.6
  864.5 3.7 copy-start.1
  901.0 3.7 copy-start.1
  937.5 3.7 copy-start.1
  974.0 3.7 copy-start.1
Sparse Core Ops, SparseCore 0:
  485.6 327.4 all-reduce.2
